TPU v7x, 512 devices: a whole 4x4x16 slice. The times are simulated.
512 devices in a mesh: pipe: 4 (over y), expert: 32 (over z, core), tensor: 4 (over x).
Axes of the slice: x: 4, y: 4, z: 16, core: 2. Of those that a mesh axis runs over, the one named last changes fastest.
Arguments:
- tokens: bfloat16 [512, 6144], P('expert', ('pipe', 'tensor')), may hold values from -6 to 6
- expert_ids: int32 [512, 2], P('expert'), may hold values from 0 to 7, all different within a row; in each aligned block of 16 rows (0 to 15, 16 to 31, ...) at most 5 rows name the same one
- gates: float32 [512, 2], P('expert'), may hold values from 0.2 to 1
- w_gate: bfloat16 [32, 6144, 2048], P('expert', None, ('pipe', 'tensor')), may hold values from -0.078125 to 0.078125
- w_up: bfloat16 [32, 6144, 2048], P('expert', None, ('pipe', 'tensor')), may hold values from -0.078125 to 0.078125
- w_down: bfloat16 [32, 2048, 6144], P('expert', ('pipe', 'tensor')), may hold values from -0.0625 to 0.0625
- d_out: bfloat16 [512, 6144], P('expert', ('pipe', 'tensor')), may hold values from -6 to 6
Outputs:
- moe_out: bfloat16 [512, 6144], P('expert', ('pipe', 'tensor'))
- grad_tokens: bfloat16 [512, 6144], P('expert', ('pipe', 'tensor'))
- grad_gates: float32 [512, 2], P('expert')
Inputs may be any that keep to these rules, and one draw needn't show every extreme that they name: `expert_ids`: each row names 2 different experts. Among the rows of one index of expert (aligned blocks of 16 rows) no expert is named more than 5 times, a bound that some block reaches.
All inputs are finite; a program needn't handle non-finite values.
Results may differ from a plain program's by a relative error of at most 0.017.
Values may be sent and summed in bfloat16 or wider, within the bound.
No kernel may reach another device: no remote copies, remote signals or barrier semaphores. Data moves between devices by JAX's collectives and lax.ppermute only.
A program may use at most 64 MiB of HBM per device.

v0:
```python
import jax
import jax.numpy as jnp
from jax import lax
from jax.sharding import PartitionSpec as P


def per_device(tokens, expert_ids, gates, w_gate, w_up, w_down, d_out):
    tok_rows = tokens.shape[0]
    top = expert_ids.shape[1]
    devices_all = lax.axis_size("expert")
    experts = min(8, devices_all)
    group = devices_all // experts
    capacity = min(
        tok_rows,
        max(2, max(5 * tok_rows * top // (4 * experts), (tok_rows * top + experts - 1) // experts)),
    )
    slots = experts * capacity
    flat_ids = expert_ids.reshape(-1)
    onehot = (flat_ids[:, None] == jnp.arange(experts, dtype=jnp.int32)[None, :]).astype(jnp.int32)
    position = jnp.sum(jnp.cumsum(onehot, axis=0) * onehot, axis=1) - 1
    slot_of = flat_ids * capacity + position
    picks = (jnp.arange(slots, dtype=jnp.int32)[:, None] == slot_of[None, :]).astype(jnp.float32)
    pick_rows = picks.reshape(slots, tok_rows, top)
    select_tok = jnp.sum(pick_rows, axis=2).astype(jnp.bfloat16)
    select_gate = jnp.sum(pick_rows * gates[None, :, :], axis=2)
    whole_x, whole_dy = (
        lax.all_gather(tokens, ("pipe", "tensor"), axis=1, tiled=True),
        lax.all_gather(d_out, ("pipe", "tensor"), axis=1, tiled=True),
    )
    picked = jnp.dot(select_tok, whole_x, preferred_element_type=jnp.float32).astype(jnp.bfloat16)
    send_x = jnp.repeat(picked.reshape(experts, capacity, -1), group, axis=0)
    scaled = jnp.dot(select_gate, whole_dy.astype(jnp.float32), precision=lax.Precision.HIGHEST)
    send_dy = jnp.repeat(scaled.astype(jnp.bfloat16).reshape(experts, capacity, -1), group, axis=0)
    recv_x, recv_dy = (
        lax.all_to_all(send_x, "expert", split_axis=0, concat_axis=0, tiled=True),
        lax.all_to_all(send_dy, "expert", split_axis=0, concat_axis=0, tiled=True),
    )
    rows_x = recv_x.reshape(devices_all * capacity, -1)
    rows_dy = recv_dy.reshape(devices_all * capacity, -1)
    gate_proj = w_gate[0]
    up_proj = w_up[0]
    down_proj = w_down[0]
    contract_last = (((1,), (1,)), ((), ()))
    h_gate = jnp.dot(rows_x, gate_proj, preferred_element_type=jnp.float32)
    h_up = jnp.dot(rows_x, up_proj, preferred_element_type=jnp.float32)
    sig = jax.nn.sigmoid(h_gate)
    hidden = (h_gate * sig * h_up).astype(jnp.bfloat16)
    out_terms = jnp.dot(hidden, down_proj, preferred_element_type=jnp.float32)
    d_hidden = lax.dot_general(
        rows_dy, down_proj, contract_last, preferred_element_type=jnp.float32
    )
    d_gate_h = (d_hidden * h_up * sig * (1.0 + h_gate * (1.0 - sig))).astype(jnp.bfloat16)
    d_up_h = (d_hidden * h_gate * sig).astype(jnp.bfloat16)
    dx_terms = lax.dot_general(
        d_gate_h, gate_proj, contract_last, preferred_element_type=jnp.float32
    )
    dx_terms = dx_terms + lax.dot_general(
        d_up_h, up_proj, contract_last, preferred_element_type=jnp.float32
    )
    out_share, dx_share = (
        lax.psum_scatter(
            out_terms.astype(jnp.bfloat16), ("pipe", "tensor"), scatter_dimension=1, tiled=True
        ).astype(jnp.float32),
        lax.psum_scatter(
            dx_terms.astype(jnp.bfloat16), ("pipe", "tensor"), scatter_dimension=1, tiled=True
        ).astype(jnp.float32),
    )
    out_slot = out_share.reshape(devices_all, capacity, -1)
    dx_slot = dx_share.reshape(devices_all, capacity, -1)
    back_out, back_dx = (
        lax.all_to_all(
            out_slot.astype(jnp.bfloat16), "expert", split_axis=0, concat_axis=0, tiled=True
        ).astype(out_slot.dtype),
        lax.all_to_all(
            dx_slot.astype(jnp.bfloat16), "expert", split_axis=0, concat_axis=0, tiled=True
        ).astype(dx_slot.dtype),
    )
    out_rows = (
        jnp.sum(back_out.reshape(experts, group, capacity, -1), axis=1)
        .astype(jnp.bfloat16)
        .reshape(slots, -1)
    )
    dx_rows = (
        jnp.sum(back_dx.reshape(experts, group, capacity, -1), axis=1)
        .astype(jnp.bfloat16)
        .reshape(slots, -1)
    )
    assign = picks.T.astype(jnp.bfloat16)
    a_out = jnp.dot(assign, out_rows, preferred_element_type=jnp.float32)
    a_dx = jnp.dot(assign, dx_rows, preferred_element_type=jnp.float32)
    a_out = a_out.reshape(tok_rows, top, -1)
    a_dx = a_dx.reshape(tok_rows, top, -1)
    moe_out = jnp.sum(gates[:, :, None] * a_out, axis=1).astype(jnp.bfloat16)
    grad_tokens = jnp.sum(a_dx, axis=1).astype(jnp.bfloat16)
    partial_dots = jnp.sum(d_out.astype(jnp.float32)[:, None, :] * a_out, axis=2)
    grad_gates = lax.psum(partial_dots, ("pipe", "tensor"))
    return (moe_out, grad_tokens, grad_gates)


def solution(mesh):
    return jax.shard_map(
        per_device,
        mesh=mesh,
        in_specs=(
            P("expert", ("pipe", "tensor")),
            P("expert", None),
            P("expert", None),
            P("expert", None, ("pipe", "tensor")),
            P("expert", None, ("pipe", "tensor")),
            P("expert", ("pipe", "tensor"), None),
            P("expert", ("pipe", "tensor")),
        ),
        out_specs=(
            P("expert", ("pipe", "tensor")),
            P("expert", ("pipe", "tensor")),
            P("expert", None),
        ),
        check_vma=False,
    )
```

profile of v0, /device:TPU:32, one launch (start us, length us, event | category | flops | bytes accessed | tf_op | source)
XLA Modules:
  0.0 613.7 jit_solution(9177753172685445268)
XLA Ops:
  9.3 24.0 %all_gather.6 = bf16[16,6144]{1,0:T(8,128)(2,1)S(1)} all-gather(bf16[16,384]{1,0:T(8,128)(2,1)} %param.7), channel_id=1, replica_groups=mesh['pipe'=4,'expert'=32,'tensor'=4] {'pipe','tensor'}, dimensions={1}, use_global_device_ids=true | all-gather | bytes 208896 | tf_op jit(solution)/shard_map/all_gather | solution.py:27
  34.7 2.0 broadcast_in_dim.4
  36.7 15.5 %all-to-all-start = ((bf16[32,5,6144]{2,1,0:T(8,128)(2,1)}), bf16[32,5,6144]{2,1,0:T(8,128)(2,1)}, u32[]{:S(2)}, u32[]{:S(2)}) async-start(bf16[32,5,6144]{2,1,0:T(8,128)(2,1)} %bitcast.42), calls=%async_computation | async-start | bytes 6291456 | tf_op jit(solution)/shard_map/all_to_all | solution.py:35
  52.2 23.1 %all_gather.7 = bf16[16,6144]{1,0:T(8,128)(2,1)S(1)} all-gather(bf16[16,384]{1,0:T(8,128)(2,1)S(1)} %copy-done.5), channel_id=1, replica_groups=mesh['pipe'=4,'expert'=32,'tensor'=4] {'pipe','tensor'}, dimensions={1}, use_global_device_ids=true | all-gather | bytes 208896 | tf_op jit(solution)/shard_map/all_gather | solution.py:28
  76.2 121.3 %all-to-all-done = bf16[32,5,6144]{2,1,0:T(8,128)(2,1)} async-done(((bf16[32,5,6144]{2,1,0:T(8,128)(2,1)}), bf16[32,5,6144]{2,1,0:T(8,128)(2,1)}, u32[]{:S(2)}, u32[]{:S(2)}) %all-to-all-start) | async-done | bytes 1966112 | tf_op jit(solution)/shard_map/all_to_all | solution.py:35
  197.5 2.1 broadcast_in_dim.5
  199.6 4.6 all-to-all-start.2
  204.2 3.0 reshape.130
  207.3 1.3 fusion.9
  208.7 1.3 fusion.5
  210.0 138.4 %all-to-all-done.2 = bf16[32,5,6144]{2,1,0:T(8,128)(2,1)} async-done(((bf16[32,5,6144]{2,1,0:T(8,128)(2,1)}), bf16[32,5,6144]{2,1,0:T(8,128)(2,1)}, u32[]{:S(2)}, u32[]{:S(2)}) %all-to-all-start.2) | async-done | bytes 1966112 | tf_op jit(solution)/shard_map/all_to_all | solution.py:36
  348.3 3.0 reshape.135
  351.4 2.1 fusion.1
  355.6 2.8 copy.34
  358.4 2.2 convolution_convert_fusion
  360.6 2.8 copy.32
  363.4 76.2 %reduce-scatter.9.cloned.1.call-done = bf16[384,160]{1,0:T(8,128)(2,1)} async-done(((bf16[6144,160]{1,0:T(8,128)(2,1)}), bf16[384,160]{1,0:T(8,128)(2,1)}) %reduce-scatter.9.cloned.1.call-update) | async-done | bytes 122896
  439.6 1.1 copy.35
  441.4 12.8 %all-to-all-start.3 = ((bf16[32,5,384]{2,1,0:T(8,128)(2,1)}), bf16[32,5,384]{2,1,0:T(8,128)(2,1)S(1)}, u32[]{:S(2)}, u32[]{:S(2)}) async-start(bf16[32,5,384]{2,1,0:T(8,128)(2,1)} %convert_element_type.142), calls=%async_computation.3 | async-start | bytes 393216 | tf_op jit(solution)/shard_map/all_to_all | solution.py:74
  454.2 80.1 %reduce-scatter.7.cloned.1.call-done = bf16[384,160]{1,0:T(8,128)(2,1)} async-done(((bf16[6144,160]{1,0:T(8,128)(2,1)}), bf16[384,160]{1,0:T(8,128)(2,1)}) %reduce-scatter.7.cloned.1.call-update) | async-done | bytes 122896
  534.3 1.1 copy.33
  536.1 12.8 %all-to-all-start.1 = ((bf16[32,5,384]{2,1,0:T(8,128)(2,1)}), bf16[32,5,384]{2,1,0:T(8,128)(2,1)S(1)}, u32[]{:S(2)}, u32[]{:S(2)}) async-start(bf16[32,5,384]{2,1,0:T(8,128)(2,1)} %convert_element_type.134), calls=%async_computation.1 | async-start | bytes 393216 | tf_op jit(solution)/shard_map/all_to_all | solution.py:71
  549.8 17.5 %all-to-all-done.1 = bf16[32,5,384]{2,1,0:T(8,128)(2,1)S(1)} async-done(((bf16[32,5,384]{2,1,0:T(8,128)(2,1)}), bf16[32,5,384]{2,1,0:T(8,128)(2,1)S(1)}, u32[]{:S(2)}, u32[]{:S(2)}) %all-to-all-start.1) | async-done | bytes 122912 | tf_op jit(solution)/shard_map/all_to_all | solution.py:71
  568.2 38.7 %psum.7 = f32[16,2]{0,1:T(2,128)} all-reduce(f32[16,2]{0,1:T(2,128)S(1)} %get-tuple-element.3), channel_id=1, replica_groups=mesh['pipe'=4,'expert'=32,'tensor'=4] {'pipe','tensor'}, use_global_device_ids=true, to_apply=%region_11.12 | all-reduce | flops 32 | bytes 256 | tf_op jit(solution)/shard_map/psum | solution.py:96
  (44 shorter events, 9.8 us)
Async XLA Ops:
  7.2 200.1 %copy-start = (bf16[1,6144,128]{2,1,0:T(8,128)(2,1)S(1)}, bf16[1,6144,128]{2,1,0:T(8,128)(2,1)}, u32[]{:S(2)}) copy-start(bf16[1,6144,128]{2,1,0:T(8,128)(2,1)} %param.10) | copy-start | bytes 4718596
  36.7 15.5 %copy-start.5 = (bf16[16,384]{1,0:T(8,128)(2,1)S(1)}, bf16[16,384]{1,0:T(8,128)(2,1)}, u32[]{:S(2)}) copy-start(bf16[16,384]{1,0:T(8,128)(2,1)} %param.13) | copy-start | bytes 36868
  36.7 160.8 %all-to-all-start = ((bf16[32,5,6144]{2,1,0:T(8,128)(2,1)}), bf16[32,5,6144]{2,1,0:T(8,128)(2,1)}, u32[]{:S(2)}, u32[]{:S(2)}) async-start(bf16[32,5,6144]{2,1,0:T(8,128)(2,1)} %bitcast.42), calls=%async_computation | async-start | bytes 6291456 | tf_op jit(solution)/shard_map/all_to_all | solution.py:35
  199.6 148.8 %all-to-all-start.2 = ((bf16[32,5,6144]{2,1,0:T(8,128)(2,1)}), bf16[32,5,6144]{2,1,0:T(8,128)(2,1)}, u32[]{:S(2)}, u32[]{:S(2)}) async-start(bf16[32,5,6144]{2,1,0:T(8,128)(2,1)} %bitcast.43), calls=%async_computation.2 | async-start | bytes 6291456 | tf_op jit(solution)/shard_map/all_to_all | solution.py:36
  204.2 235.4 %reduce-scatter.9.cloned.1.call-start = ((), (), s32[]{:S(2)}) async-start(), calls=%async_computation.7 | async-start | bytes 3342336
  207.3 1.4 copy-start.1
  351.4 2.1 copy-start.3
  351.4 2.1 copy-start.4
  353.5 1.4 copy-start.2
  358.4 175.9 %reduce-scatter.7.cloned.1.call-start = ((), (), s32[]{:S(2)}) async-start(), calls=%async_computation.6 | async-start | bytes 3342336
  363.4 203.9 %copy-start.6 = (f32[16,2]{0,1:T(2,128)S(1)}, f32[16,2]{0,1:T(2,128)}, u32[]{:S(2)}) copy-start(f32[16,2]{0,1:T(2,128)} %param.9) | copy-start | bytes 388
  441.4 94.7 %all-to-all-start.3 = ((bf16[32,5,384]{2,1,0:T(8,128)(2,1)}), bf16[32,5,384]{2,1,0:T(8,128)(2,1)S(1)}, u32[]{:S(2)}, u32[]{:S(2)}) async-start(bf16[32,5,384]{2,1,0:T(8,128)(2,1)} %convert_element_type.142), calls=%async_computation.3 | async-start | bytes 393216 | tf_op jit(solution)/shard_map/all_to_all | solution.py:74
  536.1 31.2 %all-to-all-start.1 = ((bf16[32,5,384]{2,1,0:T(8,128)(2,1)}), bf16[32,5,384]{2,1,0:T(8,128)(2,1)S(1)}, u32[]{:S(2)}, u32[]{:S(2)}) async-start(bf16[32,5,384]{2,1,0:T(8,128)(2,1)} %convert_element_type.134), calls=%async_computation.1 | async-start | bytes 393216 | tf_op jit(solution)/shard_map/all_to_all | solution.py:71
Sparse Core Ops, SparseCore 0:
  358.5 81.0 reduce-scatter.8
  443.8 90.4 reduce-scatter.6
where the time goes:
time: 615 us; the launch traced here: 614 us
  waiting for transfers between devices  433 us (70%)
  blocking collectives  85.8 us (14%)
  starting transfers between devices  45.9 us (7%)
  local copies, waits for them, and re-layouts  21.7 us (4%)
  between operations  14.3 us (2%)
  matrix products  10.8 us (2%)
    unnamed x4, waiting for transfers between devices  156 us
    all_to_all x1, waiting for transfers between devices, per_device(): lax.all_to_all(send_dy, 'expert', split_axis=0, concat_axis=0, tiled=True)  138 us
    all_to_all x1, waiting for transfers between devices, per_device(): lax.all_to_all(send_x, 'expert', split_axis=0, concat_axis=0, tiled=True)  121 us
    psum x1, blocking collectives, per_device(): grad_gates = lax.psum(partial_dots, ('pipe', 'tensor'))  38.7 us
    all_gather x1, blocking collectives, per_device(): lax.all_gather(tokens, ('pipe', 'tensor'), axis=1, tiled=True)  24 us
    all_gather x1, blocking collectives, per_device(): lax.all_gather(d_out, ('pipe', 'tensor'), axis=1, tiled=True)  23.1 us
    all_to_all x1, waiting for transfers between devices, per_device(): lax.all_to_all(out_slot.astype(jnp.bfloat16), 'expert', split_axis=0, con...  17.5 us
    all_to_all x1, starting transfers between devices, per_device(): lax.all_to_all(send_x, 'expert', split_axis=0, concat_axis=0, tiled=True)  15.5 us
  transfers between devices with their start and end apart: 6, of which 5 were waited for; matrix products, arithmetic and copies ran while one was open for 3% of the time, Pallas kernels for 0%

commit v1 on v0

--- a/solution.py
+++ b/solution.py
@@ -2,6 +2,13 @@
 import jax.numpy as jnp
 from jax import lax
 from jax.sharding import PartitionSpec as P
+
+
+def swapped_in(x, mesh_axis, dim):
+    devices = lax.axis_size(mesh_axis)
+    blocks = jnp.stack([x for _ in range(devices)])
+    blocks = lax.all_to_all(blocks, mesh_axis, split_axis=0, concat_axis=0)
+    return jnp.concatenate(blocks, axis=dim)
 
 
 def per_device(tokens, expert_ids, gates, w_gate, w_up, w_down, d_out):
@@ -24,7 +31,7 @@
     select_tok = jnp.sum(pick_rows, axis=2).astype(jnp.bfloat16)
     select_gate = jnp.sum(pick_rows * gates[None, :, :], axis=2)
     whole_x, whole_dy = (
-        lax.all_gather(tokens, ("pipe", "tensor"), axis=1, tiled=True),
+        swapped_in(tokens, ("pipe", "tensor"), 1),
         lax.all_gather(d_out, ("pipe", "tensor"), axis=1, tiled=True),
     )
     picked = jnp.dot(select_tok, whole_x, preferred_element_type=jnp.float32).astype(jnp.bfloat16)

time: 615 us -> 623 us (1.013)
  waiting for transfers between devices: 433 us -> 457 us
  blocking collectives: 85.8 us -> 62.8 us
  starting transfers between devices: 45.9 us -> 52.7 us
    all_gather x1 -> x0, blocking collectives: 24 us -> none  [per_device(): lax.all_gather(tokens, ('pipe', 'tensor'), axis=1, tiled=True)]
    all_to_all x1, waiting for transfers between devices: 121 us -> 138 us  [per_device(): lax.all_to_all(send_x, 'expert', split_axis=0, concat_axis=0, tiled=True)]
    all_to_all x1, starting transfers between devices: 15.5 us -> 4.61 us  [per_device(): lax.all_to_all(send_x, 'expert', split_axis=0, concat_axis=0, tiled=True)]
    all_to_all x1, starting transfers between devices: 4.6 us -> 15.4 us  [per_device(): lax.all_to_all(send_dy, 'expert', split_axis=0, concat_axis=0, tiled=True)]
    all_to_all x0 -> x1, starting transfers between devices: none -> 7.03 us  [swapped_in(): blocks = lax.all_to_all(blocks, mesh_axis, split_axis=0, concat_axis=0)]
    all_to_all x1, waiting for transfers between devices: 138 us -> 145 us  [per_device(): lax.all_to_all(send_dy, 'expert', split_axis=0, concat_axis=0, tiled=True)]
  transfers between devices with their start and end apart: 6 -> 7, of which waited for: 5 -> 5; matrix products, arithmetic and copies ran while one was open for 3% -> 3% of each run, Pallas kernels for 0% -> 0%
where the time goes in v1:
time: 623 us; the launch traced here: 622 us
  waiting for transfers between devices  457 us (73%)
  blocking collectives  62.8 us (10%)
  starting transfers between devices  52.7 us (8%)
  local copies, waits for them, and re-layouts  23.6 us (4%)
  between operations  14.3 us (2%)
  matrix products  10.2 us (2%)
    unnamed x4, waiting for transfers between devices  156 us
    all_to_all x1, waiting for transfers between devices, per_device(): lax.all_to_all(send_dy, 'expert', split_axis=0, concat_axis=0, tiled=True)  145 us
    all_to_all x1, waiting for transfers between devices, per_device(): lax.all_to_all(send_x, 'expert', split_axis=0, concat_axis=0, tiled=True)  138 us
    psum x1, blocking collectives, per_device(): grad_gates = lax.psum(partial_dots, ('pipe', 'tensor'))  38.7 us
    all_gather x1, blocking collectives, per_device(): lax.all_gather(d_out, ('pipe', 'tensor'), axis=1, tiled=True)  24.1 us
    all_to_all x1, waiting for transfers between devices, per_device(): lax.all_to_all(out_slot.astype(jnp.bfloat16), 'expert', split_axis=0, con...  17.4 us
    all_to_all x1, starting transfers between devices, per_device(): lax.all_to_all(send_dy, 'expert', split_axis=0, concat_axis=0, tiled=True)  15.4 us
    all_to_all x1, starting transfers between devices, per_device(): lax.all_to_all(dx_slot.astype(jnp.bfloat16), 'expert', split_axis=0, conc...  12.8 us
  transfers between devices with their start and end apart: 7, of which 5 were waited for; matrix products, arithmetic and copies ran while one was open for 3% of the time, Pallas kernels for 0%

profile of v1, /device:TPU:32, one launch (start us, length us, event | category | flops | bytes accessed | tf_op | source)
XLA Modules:
  0.0 622.1 jit_solution(15171623242345658910)
XLA Ops:
  7.2 1.5 stack.2
  8.7 7.0 %all-to-all-start = ((bf16[16,16,384]{2,1,0:T(8,128)(2,1)}), bf16[16,16,384]{2,1,0:T(8,128)(2,1)S(1)}, u32[]{:S(2)}, u32[]{:S(2)}) async-start(bf16[16,16,384]{2,1,0:T(8,128)(2,1)} %stack.2), calls=%async_computation | async-start | bytes 393216 | tf_op jit(solution)/shard_map/all_to_all | solution.py:10
  17.8 24.1 %all_gather.3 = bf16[16,6144]{1,0:T(8,128)(2,1)S(1)} all-gather(bf16[16,384]{1,0:T(8,128)(2,1)} %param.13), channel_id=1, replica_groups=mesh['pipe'=4,'expert'=32,'tensor'=4] {'pipe','tensor'}, dimensions={1}, use_global_device_ids=true | all-gather | bytes 208896 | tf_op jit(solution)/shard_map/all_gather | solution.py:35
  43.5 2.0 broadcast_in_dim.5
  45.5 15.4 %all-to-all-start.3 = ((bf16[32,5,6144]{2,1,0:T(8,128)(2,1)}), bf16[32,5,6144]{2,1,0:T(8,128)(2,1)}, u32[]{:S(2)}, u32[]{:S(2)}) async-start(bf16[32,5,6144]{2,1,0:T(8,128)(2,1)} %bitcast.45), calls=%async_computation.3 | async-start | bytes 6291456 | tf_op jit(solution)/shard_map/all_to_all | solution.py:43
  61.5 144.7 %all-to-all-done.3 = bf16[32,5,6144]{2,1,0:T(8,128)(2,1)} async-done(((bf16[32,5,6144]{2,1,0:T(8,128)(2,1)}), bf16[32,5,6144]{2,1,0:T(8,128)(2,1)}, u32[]{:S(2)}, u32[]{:S(2)}) %all-to-all-start.3) | async-done | bytes 1966112 | tf_op jit(solution)/shard_map/all_to_all | solution.py:43
  206.2 2.1 broadcast_in_dim.4
  208.2 4.6 all-to-all-start.1
  212.9 3.0 reshape.145
  215.9 2.7 fusion.1
  218.6 138.4 %all-to-all-done.1 = bf16[32,5,6144]{2,1,0:T(8,128)(2,1)} async-done(((bf16[32,5,6144]{2,1,0:T(8,128)(2,1)}), bf16[32,5,6144]{2,1,0:T(8,128)(2,1)}, u32[]{:S(2)}, u32[]{:S(2)}) %all-to-all-start.1) | async-done | bytes 1966112 | tf_op jit(solution)/shard_map/all_to_all | solution.py:42
  357.0 3.0 reshape.140
  364.2 2.8 copy.37
  367.0 2.2 convolution_convert_fusion
  369.2 2.8 copy.35
  372.0 76.1 %reduce-scatter.9.cloned.1.call-done = bf16[384,160]{1,0:T(8,128)(2,1)} async-done(((bf16[6144,160]{1,0:T(8,128)(2,1)}), bf16[384,160]{1,0:T(8,128)(2,1)}) %reduce-scatter.9.cloned.1.call-update) | async-done | bytes 122896
  448.0 1.1 copy.38
  449.8 12.8 %all-to-all-start.4 = ((bf16[32,5,384]{2,1,0:T(8,128)(2,1)}), bf16[32,5,384]{2,1,0:T(8,128)(2,1)S(1)}, u32[]{:S(2)}, u32[]{:S(2)}) async-start(bf16[32,5,384]{2,1,0:T(8,128)(2,1)} %convert_element_type.142), calls=%async_computation.4 | async-start | bytes 393216 | tf_op jit(solution)/shard_map/all_to_all | solution.py:81
  462.6 80.0 %reduce-scatter.7.cloned.1.call-done = bf16[384,160]{1,0:T(8,128)(2,1)} async-done(((bf16[6144,160]{1,0:T(8,128)(2,1)}), bf16[384,160]{1,0:T(8,128)(2,1)}) %reduce-scatter.7.cloned.1.call-update) | async-done | bytes 122896
  542.7 1.1 copy.36
  544.5 12.8 %all-to-all-start.2 = ((bf16[32,5,384]{2,1,0:T(8,128)(2,1)}), bf16[32,5,384]{2,1,0:T(8,128)(2,1)S(1)}, u32[]{:S(2)}, u32[]{:S(2)}) async-start(bf16[32,5,384]{2,1,0:T(8,128)(2,1)} %convert_element_type.134), calls=%async_computation.2 | async-start | bytes 393216 | tf_op jit(solution)/shard_map/all_to_all | solution.py:78
  558.2 17.4 %all-to-all-done.2 = bf16[32,5,384]{2,1,0:T(8,128)(2,1)S(1)} async-done(((bf16[32,5,384]{2,1,0:T(8,128)(2,1)}), bf16[32,5,384]{2,1,0:T(8,128)(2,1)S(1)}, u32[]{:S(2)}, u32[]{:S(2)}) %all-to-all-start.2) | async-done | bytes 122912 | tf_op jit(solution)/shard_map/all_to_all | solution.py:78
  575.7 0.9 multiply_reduce_fusion
  576.6 38.7 %psum.7 = f32[16,2]{0,1:T(2,128)} all-reduce(f32[16,2]{0,1:T(2,128)S(1)} %get-tuple-element.3), channel_id=1, replica_groups=mesh['pipe'=4,'expert'=32,'tensor'=4] {'pipe','tensor'}, use_global_device_ids=true, to_apply=%region_11.12 | all-reduce | flops 32 | bytes 256 | tf_op jit(solution)/shard_map/psum | solution.py:103
  (47 shorter events, 10.7 us)
Async XLA Ops:
  7.2 352.9 %copy-start = (bf16[1,6144,128]{2,1,0:T(8,128)(2,1)S(1)}, bf16[1,6144,128]{2,1,0:T(8,128)(2,1)}, u32[]{:S(2)}) copy-start(bf16[1,6144,128]{2,1,0:T(8,128)(2,1)} %param.10) | copy-start | bytes 4718596
  8.7 34.8 %all-to-all-start = ((bf16[16,16,384]{2,1,0:T(8,128)(2,1)}), bf16[16,16,384]{2,1,0:T(8,128)(2,1)S(1)}, u32[]{:S(2)}, u32[]{:S(2)}) async-start(bf16[16,16,384]{2,1,0:T(8,128)(2,1)} %stack.2), calls=%async_computation | async-start | bytes 393216 | tf_op jit(solution)/shard_map/all_to_all | solution.py:10
  45.5 160.7 %all-to-all-start.3 = ((bf16[32,5,6144]{2,1,0:T(8,128)(2,1)}), bf16[32,5,6144]{2,1,0:T(8,128)(2,1)}, u32[]{:S(2)}, u32[]{:S(2)}) async-start(bf16[32,5,6144]{2,1,0:T(8,128)(2,1)} %bitcast.45), calls=%async_computation.3 | async-start | bytes 6291456 | tf_op jit(solution)/shard_map/all_to_all | solution.py:43
  208.2 148.8 %all-to-all-start.1 = ((bf16[32,5,6144]{2,1,0:T(8,128)(2,1)}), bf16[32,5,6144]{2,1,0:T(8,128)(2,1)}, u32[]{:S(2)}, u32[]{:S(2)}) async-start(bf16[32,5,6144]{2,1,0:T(8,128)(2,1)} %bitcast.46), calls=%async_computation.1 | async-start | bytes 6291456 | tf_op jit(solution)/shard_map/all_to_all | solution.py:42
  212.8 235.2 %reduce-scatter.9.cloned.1.call-start = ((), (), s32[]{:S(2)}) async-start(), calls=%async_computation.8 | async-start | bytes 3342336
  360.0 1.4 copy-start.1
  361.4 2.0 copy-start.2
  361.4 1.3 copy-start.4
  362.1 0.6 copy-start.3
  366.9 175.7 %reduce-scatter.7.cloned.1.call-start = ((), (), s32[]{:S(2)}) async-start(), calls=%async_computation.7 | async-start | bytes 3342336
  371.9 185.3 %copy-start.5 = (bf16[16,384]{1,0:T(8,128)(2,1)S(1)}, bf16[16,384]{1,0:T(8,128)(2,1)}, u32[]{:S(2)}) copy-start(bf16[16,384]{1,0:T(8,128)(2,1)} %param.13) | copy-start | bytes 36868
  372.0 203.7 %copy-start.6 = (f32[16,2]{0,1:T(2,128)S(1)}, f32[16,2]{0,1:T(2,128)}, u32[]{:S(2)}) copy-start(f32[16,2]{0,1:T(2,128)} %param.9) | copy-start | bytes 388
  449.8 94.6 %all-to-all-start.4 = ((bf16[32,5,384]{2,1,0:T(8,128)(2,1)}), bf16[32,5,384]{2,1,0:T(8,128)(2,1)S(1)}, u32[]{:S(2)}, u32[]{:S(2)}) async-start(bf16[32,5,384]{2,1,0:T(8,128)(2,1)} %convert_element_type.142), calls=%async_computation.4 | async-start | bytes 393216 | tf_op jit(solution)/shard_map/all_to_all | solution.py:81
  544.5 31.1 %all-to-all-start.2 = ((bf16[32,5,384]{2,1,0:T(8,128)(2,1)}), bf16[32,5,384]{2,1,0:T(8,128)(2,1)S(1)}, u32[]{:S(2)}, u32[]{:S(2)}) async-start(bf16[32,5,384]{2,1,0:T(8,128)(2,1)} %convert_element_type.134), calls=%async_computation.2 | async-start | bytes 393216 | tf_op jit(solution)/shard_map/all_to_all | solution.py:78
Sparse Core Ops, SparseCore 0:
  367.1 80.9 reduce-scatter.8
  452.2 90.3 reduce-scatter.6
